TPU v7x, 256 devices: a whole 4x4x8 slice. The times are simulated.
256 devices in a mesh: section: 2 (over core), seq: 32 (over z, x), cfg: 4 (over y).
Axes of the slice: x: 4, y: 4, z: 8, core: 2. Of those that a mesh axis runs over, the one named last changes fastest.
Arguments:
- hidden_states: bfloat16 [4, 4, 512, 3072], P('cfg', None, 'seq'), may hold values from -250 to 250
- latent: float32 [2, 4, 512, 64], P('section', None, 'seq'), may hold values from -6 to 6
- stale_cache: bfloat16 [2, 4, 32, 2048, 128], P('section', 'cfg', 'seq'), may hold values from -140 to 140
- qkv_weight: bfloat16 [2, 3072, 3, 2048], P('section', None, None, 'cfg'), may hold values from -0.109375 to 0.109375
- out_weight: bfloat16 [2, 3072, 2048], P('section', 'seq', 'cfg'), may hold values from -0.125 to 0.125
- modulation: float32 [2, 6, 3072], P('section'), may hold values from -2.5 to 2.5
- out_modulation: float32 [2, 3072], replicated, may hold values from -2.5 to 2.5
- proj_weight: bfloat16 [3072, 64], replicated, may hold values from -0.109375 to 0.109375
- solver_coef: float32 [2, 3], P('section'), may hold values from 0.5 to 2
- video_len: int32 [2], replicated, may hold values from 911 to 1822, as said below
- text_len: int32 [4], replicated, may hold values from 1 to 226, as said below
- positions: int32 [3, 2, 4, 512], P(None, None, None, 'seq'), may hold values from 0 to 47
Outputs:
- new_latent: float32 [2, 4, 512, 64], P('section', None, 'seq')
- new_cache: bfloat16 [2, 4, 32, 2048, 128], P('section', 'cfg', 'seq')
Inputs may be any that keep to these rules, and one draw needn't show every extreme that they name: `video_len`: in every draw one request has exactly 1822 video tokens. `text_len`: in every draw some sequence has all 226 text tokens live.
All inputs are finite; a program needn't handle non-finite values.
Results may differ from a plain program's by a relative error of at most 0.02.
Values may be sent and summed in bfloat16 or wider, within the bound.
No kernel may reach another device: no remote copies, remote signals or barrier semaphores. Data moves between devices by JAX's collectives and lax.ppermute only.
A program may use at most 128 MiB of HBM per device.

v0:
```python
import math

import jax
import jax.numpy as jnp
from jax import lax
from jax.experimental import pallas as pl
from jax.sharding import PartitionSpec as P

HD = 64
TEXT = 226


def from_behind(value, axis, steps):
    count = lax.axis_size(axis)
    pairs = [(source, (source + steps) % count) for source in range(count)]
    return lax.ppermute(value, axis, pairs)


def row_norm(values):
    centered = values - jnp.mean(values, axis=-1, keepdims=True)
    return centered * lax.rsqrt(jnp.mean(centered * centered, axis=-1, keepdims=True) + 1e-05)


def head_norm(values):
    centered = values - jnp.mean(values, axis=-1, keepdims=True)
    return centered * lax.rsqrt(jnp.mean(centered * centered, axis=-1, keepdims=True) + 1e-06)


def rope_angles(places, head_size):
    half_size = head_size // 2
    pairs_t = head_size // 8
    pairs_h = (half_size - pairs_t) // 2
    pair_index = jnp.arange(half_size)
    first_part = pair_index < pairs_t
    second_part = jnp.logical_and(pair_index >= pairs_t, pair_index < pairs_t + pairs_h)
    third_part = pair_index >= pairs_t + pairs_h
    local_index = jnp.where(
        first_part,
        pair_index,
        jnp.where(second_part, pair_index - pairs_t, pair_index - pairs_t - pairs_h),
    )
    axis_span = jnp.where(first_part, 2 * pairs_t, 2 * pairs_h)
    frequency = jnp.exp(
        -math.log(10000.0) * 2.0 * local_index.astype(jnp.float32) / axis_span.astype(jnp.float32)
    )
    angles = places[0][..., None] * first_part.astype(jnp.float32)
    angles = angles + places[1][..., None] * second_part.astype(jnp.float32)
    angles = angles + places[2][..., None] * third_part.astype(jnp.float32)
    return angles * frequency


def rotate(values, cos_table, sin_table):
    half_size = values.shape[-1] // 2
    first_half = values[..., :half_size]
    second_half = values[..., half_size:]
    return jnp.concatenate(
        [
            first_half * cos_table - second_half * sin_table,
            second_half * cos_table + first_half * sin_table,
        ],
        axis=-1,
    )


def shift_within(value, active, steps):
    count = lax.axis_size("cfg")
    pairs = [
        (active * count + source, active * count + (source + steps) % count)
        for source in range(count)
    ]
    return lax.ppermute(value, ("section", "cfg"), pairs)


def gather_cfg(values, active):
    count = lax.axis_size("cfg")
    here = lax.axis_index("cfg")
    slots = [values] + [shift_within(values, active, shift) for shift in range(1, count)]
    ordered = jnp.concatenate(slots[::-1], axis=0)
    return jnp.roll(ordered, here + 1, axis=0)


def scatter_cfg(partials, active):
    count = lax.axis_size("cfg")
    here = lax.axis_index("cfg")
    total = lax.dynamic_index_in_dim(partials, here, 0, keepdims=True)
    for shift in range(1, count):
        outgoing = lax.dynamic_index_in_dim(partials, (here + shift) % count, 0, keepdims=True)
        outgoing = outgoing.astype(jnp.bfloat16)
        total = total + shift_within(outgoing, active, shift).astype(jnp.float32)
    return total


def attend_kernel(query_ref, fresh_key_ref, fresh_value_ref, stale_key_ref, stale_value_ref, live_ref, out_ref):
    patch_id = pl.program_id(0) // 2
    patch_len = 2 * query_ref.shape[1]
    total_len = fresh_key_ref.shape[0]
    key_patch = lax.broadcasted_iota(jnp.int32, (total_len, 1), 0) // patch_len
    use_fresh = key_patch <= patch_id
    key_rows = jnp.where(use_fresh, fresh_key_ref[...], stale_key_ref[...])
    value_rows = jnp.where(use_fresh, fresh_value_ref[...], stale_value_ref[...])
    scores = lax.dot_general(
        query_ref[0] * jnp.asarray(HD ** (-0.5), query_ref.dtype),
        key_rows,
        (((1,), (1,)), ((), ())),
        preferred_element_type=jnp.float32,
    )
    scores = jnp.where(live_ref[...] > 0, scores, -jnp.inf)
    row_max = jnp.max(scores, axis=1, keepdims=True)
    weights = jnp.exp(scores - row_max)
    row_sum = jnp.sum(weights, axis=1, keepdims=True)
    combined = jnp.dot(
        weights.astype(jnp.bfloat16), value_rows, preferred_element_type=jnp.float32
    )
    out_ref[0] = (combined / row_sum).astype(out_ref.dtype)


def attend(queries, fresh_keys, fresh_values, stale_keys, stale_values, live_flags):
    patches, patch_len, head_size = queries.shape
    total_len = fresh_keys.shape[0]
    return pl.pallas_call(
        attend_kernel,
        grid=(2 * patches,),
        in_specs=[
            pl.BlockSpec((1, patch_len // 2, head_size), lambda p: (p // 2, p % 2, 0)),
            pl.BlockSpec((total_len, head_size), lambda p: (0, 0)),
            pl.BlockSpec((total_len, head_size), lambda p: (0, 0)),
            pl.BlockSpec((total_len, head_size), lambda p: (0, 0)),
            pl.BlockSpec((total_len, head_size), lambda p: (0, 0)),
            pl.BlockSpec((1, total_len), lambda p: (0, 0)),
        ],
        out_specs=pl.BlockSpec((1, patch_len // 2, head_size), lambda p: (p // 2, p % 2, 0)),
        out_shape=jax.ShapeDtypeStruct(queries.shape, jnp.bfloat16),
    )(queries, fresh_keys, fresh_values, stale_keys, stale_values, live_flags)


def per_device(
    hidden_states,
    latent,
    stale_cache,
    qkv_weight,
    out_weight,
    modulation,
    out_modulation,
    proj_weight,
    solver_coef,
    video_len,
    text_len,
    positions,
):
    section_id = lax.axis_index("section")
    shard_id = lax.axis_index("seq")
    seq_devices = lax.axis_size("seq")
    cfg_devices = lax.axis_size("cfg")
    patches = hidden_states.shape[1]
    patch_dev = hidden_states.shape[2]
    width = hidden_states.shape[3]
    patch_len = patch_dev * seq_devices
    total_len = patch_len * patches
    group_heads = qkv_weight.shape[3] // HD
    seq_count = cfg_devices
    qkv_full = qkv_weight[0].reshape(width, 3 * group_heads * HD)
    out_full = lax.all_gather(out_weight[0], "seq", axis=0, tiled=True).reshape(
        width, group_heads, HD
    )
    mod_rows = modulation[0]
    stale_rows = stale_cache[0, 0, 0]
    stale_keys = stale_rows[:, :HD]
    stale_values = stale_rows[:, HD:]
    my_sequence = shard_id // group_heads
    row_ids = jnp.arange(total_len)
    text_limit = lax.dynamic_index_in_dim(text_len, my_sequence, keepdims=False)
    video_limit = lax.dynamic_index_in_dim(video_len, my_sequence // 2, keepdims=False)
    live_keys = jnp.where(row_ids < TEXT, row_ids < text_limit, row_ids - TEXT < video_limit)
    live_flags = live_keys.astype(jnp.int32)[None, :]
    scale_factor = HD ** (-0.5)

    row_place = (
        jnp.arange(patches)[:, None] * patch_len
        + shard_id * patch_dev
        + jnp.arange(patch_dev)[None, :]
    )
    text_rows = (row_place < TEXT)[:, :, None]
    shift_rows = jnp.where(text_rows, mod_rows[3], mod_rows[0])
    scale_rows = jnp.where(text_rows, mod_rows[4], mod_rows[1])
    gate_rows = jnp.where(text_rows, mod_rows[5], mod_rows[2])
    angles = rope_angles(positions.astype(jnp.float32), HD)
    angles = jnp.where(text_rows[None], 0.0, angles)
    angles = jnp.repeat(angles, 2, axis=0)[:, None]
    cos_table = jnp.cos(angles)
    sin_table = jnp.sin(angles)

    def run(hidden, active):
        normed = row_norm(hidden.astype(jnp.float32))
        mixed_rows = (normed * (1.0 + scale_rows) + shift_rows).astype(jnp.bfloat16)
        mixed_rows = gather_cfg(mixed_rows, active)
        projected = jnp.dot(
            mixed_rows.reshape(-1, width), qkv_full, preferred_element_type=jnp.float32
        )
        projected = projected.reshape(seq_count, patches, patch_dev, 3, group_heads, HD)
        projected = projected.transpose(0, 4, 3, 1, 2, 5)
        queries = rotate(head_norm(projected[:, :, 0]), cos_table, sin_table)
        key_part = rotate(head_norm(projected[:, :, 1]), cos_table, sin_table)
        stacked = jnp.stack([queries, key_part, projected[:, :, 2]], axis=2).astype(jnp.bfloat16)
        outgoing = stacked.reshape(seq_count * group_heads, 3, patches, patch_dev * HD)
        incoming = lax.all_to_all(outgoing, "seq", split_axis=0, concat_axis=3, tiled=True)
        incoming = incoming.reshape(3, patches, patch_len, HD)
        fresh_rows = jnp.concatenate([incoming[1], incoming[2]], axis=-1).reshape(
            total_len, 2 * HD
        )
        attended = attend(
            incoming[0],
            incoming[1].reshape(total_len, HD),
            incoming[2].reshape(total_len, HD),
            stale_keys,
            stale_values,
            live_flags,
        )
        attended = attended.reshape(patches, seq_devices, patch_dev * HD)[None]
        returned = lax.all_to_all(attended, "seq", split_axis=2, concat_axis=0, tiled=True)
        returned = returned.reshape(seq_count, group_heads, patches, patch_dev, HD)
        update = scatter_cfg(
            jnp.einsum("sgpqe,dge->spqd", returned, out_full, preferred_element_type=jnp.float32),
            active,
        )
        result = (hidden.astype(jnp.float32) + gate_rows * update).astype(jnp.bfloat16)
        return result, fresh_rows

    first_out, first_cache = run(hidden_states, 0)
    received = from_behind(first_out, "section", 1)
    second_out, second_cache = run(received, 1)
    key_cache = jnp.where(section_id == 0, first_cache, second_cache)

    normed = row_norm(second_out.astype(jnp.float32))
    normed_out = (normed * (1.0 + out_modulation[1]) + out_modulation[0]).astype(jnp.bfloat16)
    predicted = jnp.einsum(
        "spqd,do->spqo", normed_out, proj_weight, preferred_element_type=jnp.float32
    )
    count = cfg_devices
    here = lax.axis_index("cfg")
    slots = []
    for step in range(count):
        pairs = [(count, step), (count + 1, (step + 1) % count)]
        if step < count - 1:
            pairs += [(count + 2, count + (3 + step) % count), (count + 3, count + step)]
        slots.append(lax.ppermute(predicted, ("section", "cfg"), pairs))
    slots = jnp.concatenate(slots, axis=0)
    first_table = jnp.array([1, 2, 0, 0], jnp.int32)
    second_table = jnp.array([0, 1, 2, 0], jnp.int32)
    first_at = jnp.where(section_id == 0, here, first_table[here])
    second_at = jnp.where(section_id == 0, (here + count - 1) % count, second_table[here])
    first_rows = lax.dynamic_index_in_dim(slots, first_at, 0, keepdims=False)
    second_rows = lax.dynamic_index_in_dim(slots, second_at, 0, keepdims=False)
    first_rows = jnp.where((section_id == 1) & (here == 2), predicted[0], first_rows)
    second_rows = jnp.where((section_id == 1) & (here == 3), predicted[0], second_rows)
    pair_rows = jnp.stack([first_rows, second_rows], axis=0)
    solver_row = solver_coef[0]
    guided = pair_rows[0] + solver_row[2] * (pair_rows[1] - pair_rows[0])
    new_latent = solver_row[0] * latent[0] + solver_row[1] * guided
    return (new_latent[None], key_cache[None, None, None])


def solution(mesh):
    return jax.shard_map(
        per_device,
        mesh=mesh,
        in_specs=(
            P("cfg", None, "seq", None),
            P("section", None, "seq", None),
            P("section", "cfg", "seq", None, None),
            P("section", None, None, "cfg"),
            P("section", "seq", "cfg"),
            P("section", None, None),
            P(),
            P(),
            P("section", None),
            P(),
            P(),
            P(None, None, None, "seq"),
        ),
        out_specs=(P("section", None, "seq", None), P("section", "cfg", "seq", None, None)),
        check_vma=False,
    )
```

profile of v0, /device:TPU:1, one launch (start us, length us, event | category | flops | bytes accessed | tf_op | source)
XLA Modules:
  0.0 280.7 jit_solution(3750612398579650133)
XLA Ops:
  15.3 12.7 %copy.31 = bf16[1,3072,3,512]{1,3,2,0:T(8,128)(2,1)} copy(bf16[1,3072,3,512]{3,1,2,0:T(8,128)(2,1)} %param.19) | data formatting | bytes 18874368 | tf_op args[3]
  28.4 9.8 %convolution_bitcast_fusion.3 = f32[4,8,3,4,16,64]{5,4,1,2,3,0:T(8,128)S(1)} fusion(bf16[3,8,64,3072,1,1]{3,2,1,0,5,4:T(8,128)(2,1)} %bitcast.187, s32[]{:T(128)S(6)} %select_n.209, bf16[1,4,16,3072]{3,2,1,0:T(8,128)(2,1)S(1)} %collective-permute-done, bf16[1,4,16,3072]{3,2,1,0:T(8,128)(2,1)S(1)} %collective-permute-done.1, ...), kind=kOutput, calls=%fused_computation.19 | convolution fusion | flops 2428502016 | bytes 12582916 | tf_op jit(solution)/shard_map/dot_general | solution.py:196
  45.9 12.0 %all-to-all-start = ((bf16[32,3,4,1024]{3,2,1,0:T(4,128)(2,1)}), bf16[32,3,4,1024]{3,2,1,0:T(4,128)(2,1)S(1)}, u32[]{:S(2)}, u32[]{:S(2)}) async-start(bf16[32,3,4,1024]{3,2,1,0:T(4,128)(2,1)} %copy.36), calls=%async_computation | async-start | bytes 1572864 | tf_op jit(solution)/shard_map/all_to_all | solution.py:205
  59.2 1.9 select_convert_fusion.live_ref
  62.3 10.5 %all-to-all-done = bf16[32,3,4,1024]{3,2,1,0:T(4,128)(2,1)S(1)} async-done(((bf16[32,3,4,1024]{3,2,1,0:T(4,128)(2,1)}), bf16[32,3,4,1024]{3,2,1,0:T(4,128)(2,1)S(1)}, u32[]{:S(2)}, u32[]{:S(2)}) %all-to-all-start) | async-done | bytes 786464 | tf_op jit(solution)/shard_map/all_to_all | solution.py:205
  76.8 12.5 %shard_map.149 = bf16[4,512,64]{2,1,0:T(8,128)(2,1)} custom-call(bf16[4,512,64]{2,1,0:T(8,128)(2,1)} %squeeze.92.query_ref, bf16[2048,64]{1,0:T(8,128)(2,1)} %reshape_squeeze.16.fresh_key_ref, bf16[2048,64]{1,0:T(8,128)(2,1)} %reshape_squeeze.17.fresh_value_ref, bf16[2048,64]{1,0:T(8,128)(2,1)} %get-tuple-element.36.stale_key_ref, ...), custom_call_target="tpu_custom_call" | custom-call | tf_op jit(solution)/shard_map/pallas_call | solution.py:120
  91.7 4.9 %all-to-all-start.1 = ((bf16[1,4,32,1024]{3,1,0,2:T(4,128)(2,1)}), bf16[1,4,32,1024]{3,1,0,2:T(4,128)(2,1)S(1)}, u32[]{:S(2)}, u32[]{:S(2)}) async-start(bf16[1,4,32,1024]{3,1,0,2:T(4,128)(2,1)} %copy.40), calls=%async_computation.1 | async-start | bytes 524288 | tf_op jit(solution)/shard_map/all_to_all | solution.py:219
  96.6 10.9 %all-to-all-done.1 = bf16[1,4,32,1024]{3,1,0,2:T(4,128)(2,1)S(1)} async-done(((bf16[1,4,32,1024]{3,1,0,2:T(4,128)(2,1)}), bf16[1,4,32,1024]{3,1,0,2:T(4,128)(2,1)S(1)}, u32[]{:S(2)}, u32[]{:S(2)}) %all-to-all-start.1) | async-done | bytes 262176 | tf_op jit(solution)/shard_map/all_to_all | solution.py:219
  107.9 4.6 %copy.42 = bf16[1,3072,512]{1,2,0:T(8,128)(2,1)} copy(bf16[1,3072,512]{2,1,0:T(8,128)(2,1)} %all-gather.3.cloned.1.call-done) | data formatting | bytes 6291456 | tf_op jit(solution)/shard_map/all_gather | solution.py:162
  112.5 3.0 %convolution_bitcast_fusion.1 = f32[4,4,16,3072]{3,2,1,0:T(8,128)S(1)} fusion(bf16[4,8,4,16,64]{4,3,2,1,0:T(8,128)(2,1)S(1)} %reshape.441, bf16[3072,8,64,1,1]{0,2,4,1,3:T(8,128)(2,1)} %bitcast.189), kind=kOutput, calls=%fused_computation.1 | convolution fusion | flops 805306368 | bytes 6553600 | tf_op jit(solution)/shard_map/sgpqe,dge->spqd/dot_general | solution.py:222
  115.5 1.6 copy-done.4
  121.7 26.5 %collective-permute-start.6 = (bf16[1,4,16,3072]{3,2,1,0:T(8,128)(2,1)S(1)}, bf16[1,4,16,3072]{3,2,1,0:T(8,128)(2,1)S(1)}, u32[]{:S(2)}, u32[]{:S(2)}) collective-permute-start(bf16[1,4,16,3072]{3,2,1,0:T(8,128)(2,1)S(1)} %fusion.40), channel_id=1, source_target_pairs={{0,128},{128,0},{1,129},{129,1},{2,130},{130,2},{3,131},{131,3},{4... | collective-permute-start | bytes 1179656 | tf_op jit(solution)/shard_map/ppermute | solution.py:16
  150.2 4.3 %collective-permute-start.7 = (bf16[1,4,16,3072]{3,2,1,0:T(8,128)(2,1)S(1)}, bf16[1,4,16,3072]{3,2,1,0:T(8,128)(2,1)S(1)}, u32[]{:S(2)}, u32[]{:S(2)}) collective-permute-start(bf16[1,4,16,3072]{3,2,1,0:T(8,128)(2,1)S(1)} %fusion.39), channel_id=1, source_target_pairs={{128,131},{129,128},{130,129},{131,130},{132,135},{133,132},{134,1... | collective-permute-start | bytes 1179656 | tf_op jit(solution)/shard_map/ppermute | solution.py:71
  154.5 2.9 %collective-permute-start.8 = (bf16[1,4,16,3072]{3,2,1,0:T(8,128)(2,1)S(1)}, bf16[1,4,16,3072]{3,2,1,0:T(8,128)(2,1)S(1)}, u32[]{:S(2)}, u32[]{:S(2)}) collective-permute-start(bf16[1,4,16,3072]{3,2,1,0:T(8,128)(2,1)S(1)} %fusion.39), channel_id=1, source_target_pairs={{128,130},{129,131},{130,128},{131,129},{132,134},{133,135},{134,1... | collective-permute-start | bytes 1179656 | tf_op jit(solution)/shard_map/ppermute | solution.py:71
  157.5 2.1 collective-permute-start.9
  159.6 3.8 %collective-permute-done.7 = bf16[1,4,16,3072]{3,2,1,0:T(8,128)(2,1)S(1)} collective-permute-done((bf16[1,4,16,3072]{3,2,1,0:T(8,128)(2,1)S(1)}, bf16[1,4,16,3072]{3,2,1,0:T(8,128)(2,1)S(1)}, u32[]{:S(2)}, u32[]{:S(2)}) %collective-permute-start.7) | collective-permute-done | bytes 393248 | tf_op jit(solution)/shard_map/ppermute | solution.py:71
  164.7 4.1 %collective-permute-done.9 = bf16[1,4,16,3072]{3,2,1,0:T(8,128)(2,1)S(1)} collective-permute-done((bf16[1,4,16,3072]{3,2,1,0:T(8,128)(2,1)S(1)}, bf16[1,4,16,3072]{3,2,1,0:T(8,128)(2,1)S(1)}, u32[]{:S(2)}, u32[]{:S(2)}) %collective-permute-start.9) | collective-permute-done | bytes 393248 | tf_op jit(solution)/shard_map/ppermute | solution.py:71
  168.8 9.7 %convolution_bitcast_fusion.2 = f32[4,8,3,4,16,64]{5,4,1,3,0,2:T(8,128)S(1)} fusion(bf16[3,8,64,3072,1,1]{3,2,1,5,4,0:T(8,128)(2,1)} %bitcast.188, s32[]{:T(128)S(6)} %select_n.209, bf16[1,4,16,3072]{3,2,1,0:T(8,128)(2,1)S(1)} %collective-permute-done.7, bf16[1,4,16,3072]{3,2,1,0:T(8,128)(2,1)S(1)} %collective-permute-done.8, ...), kind=kOutput, calls=%fused_computation.18 | convolution fusion | flops 2428502016 | bytes 12582916 | tf_op jit(solution)/shard_map/dot_general | solution.py:196
  185.9 18.2 %all_to_all.60 = bf16[32,3,4,1024]{3,2,1,0:T(4,128)(2,1)S(1)} all-to-all(bf16[32,3,4,1024]{3,2,1,0:T(4,128)(2,1)S(1)} %copy.48), channel_id=1, replica_groups=mesh['section'=2,'seq'=32,'cfg'=4] {'seq'}, dimensions={0} | all-to-all | bytes 1572864 | tf_op jit(solution)/shard_map/all_to_all | solution.py:205
  208.2 12.4 %shard_map.150 = bf16[4,512,64]{2,1,0:T(8,128)(2,1)} custom-call(bf16[4,512,64]{2,1,0:T(8,128)(2,1)} %squeeze.99.query_ref, bf16[2048,64]{1,0:T(8,128)(2,1)} %reshape_squeeze.18.fresh_key_ref, bf16[2048,64]{1,0:T(8,128)(2,1)} %reshape_squeeze.19.fresh_value_ref, bf16[2048,64]{1,0:T(8,128)(2,1)} %get-tuple-element.36.stale_key_ref, ...), custom_call_target="tpu_custom_call" | custom-call | tf_op jit(solution)/shard_map/pallas_call | solution.py:120
  223.0 4.7 %all-to-all-start.3 = ((bf16[1,4,32,1024]{3,1,0,2:T(4,128)(2,1)}), bf16[1,4,32,1024]{3,1,0,2:T(4,128)(2,1)S(1)}, u32[]{:S(2)}, u32[]{:S(2)}) async-start(bf16[1,4,32,1024]{3,1,0,2:T(4,128)(2,1)} %copy.52), calls=%async_computation.3 | async-start | bytes 524288 | tf_op jit(solution)/shard_map/all_to_all | solution.py:219
  230.7 7.3 %all-to-all-done.3 = bf16[1,4,32,1024]{3,1,0,2:T(4,128)(2,1)S(1)} async-done(((bf16[1,4,32,1024]{3,1,0,2:T(4,128)(2,1)}), bf16[1,4,32,1024]{3,1,0,2:T(4,128)(2,1)S(1)}, u32[]{:S(2)}, u32[]{:S(2)}) %all-to-all-start.3) | async-done | bytes 262176 | tf_op jit(solution)/shard_map/all_to_all | solution.py:219
  238.5 2.9 %convolution_bitcast_fusion = f32[4,4,16,3072]{3,2,1,0:T(8,128)S(1)} fusion(bf16[4,8,4,16,64]{4,3,2,1,0:T(8,128)(2,1)S(1)} %reshape.442, bf16[3072,8,64,1,1]{0,2,4,1,3:T(8,128)(2,1)} %bitcast.190), kind=kOutput, calls=%fused_computation | convolution fusion | flops 805306368 | bytes 6553600 | tf_op jit(solution)/shard_map/sgpqe,dge->spqd/dot_general | solution.py:222
  242.6 1.9 collective-permute-start.10
  244.5 3.4 %collective-permute-start.11 = (bf16[1,4,16,3072]{3,2,1,0:T(8,128)(2,1)}, bf16[1,4,16,3072]{3,2,1,0:T(8,128)(2,1)}, u32[]{:S(2)}, u32[]{:S(2)}) collective-permute-start(bf16[1,4,16,3072]{3,2,1,0:T(8,128)(2,1)} %get-tuple-element.13), channel_id=1, source_target_pairs={{128,130},{129,131},{130,128},{131,129},{132,134},{133,135},{134,1... | collective-permute-start | bytes 1179656 | tf_op jit(solution)/shard_map/ppermute | solution.py:71
  247.8 3.5 %collective-permute-start.12 = (bf16[1,4,16,3072]{3,2,1,0:T(8,128)(2,1)}, bf16[1,4,16,3072]{3,2,1,0:T(8,128)(2,1)}, u32[]{:S(2)}, u32[]{:S(2)}) collective-permute-start(bf16[1,4,16,3072]{3,2,1,0:T(8,128)(2,1)} %get-tuple-element.12), channel_id=1, source_target_pairs={{128,131},{129,128},{130,129},{131,130},{132,135},{133,132},{134,1... | collective-permute-start | bytes 1179656 | tf_op jit(solution)/shard_map/ppermute | solution.py:71
  252.9 3.9 %collective-permute-done.10 = bf16[1,4,16,3072]{3,2,1,0:T(8,128)(2,1)} collective-permute-done((bf16[1,4,16,3072]{3,2,1,0:T(8,128)(2,1)}, bf16[1,4,16,3072]{3,2,1,0:T(8,128)(2,1)}, u32[]{:S(2)}, u32[]{:S(2)}) %collective-permute-start.10) | collective-permute-done | bytes 393248 | tf_op jit(solution)/shard_map/ppermute | solution.py:71
  256.8 2.5 collective-permute-done.12
  259.3 1.9 convert_reduce_fusion.2
  261.9 1.9 collective-permute-start.13
  265.2 1.9 collective-permute-start.14
  271.4 2.5 fusion.57
  (169 shorter events, 57.3 us)
Async XLA Ops:
  7.2 254.3 %copy-start = (bf16[3072,64]{0,1:T(8,128)(2,1)S(1)}, bf16[3072,64]{0,1:T(8,128)(2,1)}, u32[]{:S(2)}) copy-start(bf16[3072,64]{0,1:T(8,128)(2,1)} %param.23) | copy-start | bytes 1179652
  7.2 100.7 %all-gather.3.cloned.1.call-start = ((), (), s32[]{:S(2)}) async-start(), calls=%async_computation.4 | async-start | bytes 3244032 | tf_op jit(solution)/shard_map/all_gather | solution.py:162
  8.7 19.3 %copy-start.9 = (f32[1,1,3072]{2,0,1:T(1,128)}, f32[1,1,3072]{2,0,1:T(1,128)S(1)}, u32[]{:S(2)}) copy-start(f32[1,1,3072]{2,0,1:T(1,128)S(1)} %get-tuple-element.43) | copy-start | bytes 36868
  8.7 19.3 %copy-start.11 = (f32[1,1,3072]{2,0,1:T(1,128)}, f32[1,1,3072]{2,0,1:T(1,128)S(1)}, u32[]{:S(2)}) copy-start(f32[1,1,3072]{2,0,1:T(1,128)S(1)} %get-tuple-element.45) | copy-start | bytes 36868
  8.7 19.3 %copy-start.13 = (f32[1,1,3072]{2,0,1:T(1,128)}, f32[1,1,3072]{2,0,1:T(1,128)S(1)}, u32[]{:S(2)}) copy-start(f32[1,1,3072]{2,0,1:T(1,128)S(1)} %get-tuple-element.46) | copy-start | bytes 36868
  12.4 16.0 %collective-permute-start = (bf16[1,4,16,3072]{3,2,1,0:T(8,128)(2,1)S(1)}, bf16[1,4,16,3072]{3,2,1,0:T(8,128)(2,1)S(1)}, u32[]{:S(2)}, u32[]{:S(2)}) collective-permute-start(bf16[1,4,16,3072]{3,2,1,0:T(8,128)(2,1)S(1)} %fusion.38), channel_id=1, source_target_pairs={{0,3},{1,0},{2,1},{3,2},{4,7},{5,4},{6,5},{7,6},{8,11},{9,8},{10,9... | collective-permute-start | bytes 1179656 | tf_op jit(solution)/shard_map/ppermute | solution.py:71
  13.1 15.3 %collective-permute-start.1 = (bf16[1,4,16,3072]{3,2,1,0:T(8,128)(2,1)S(1)}, bf16[1,4,16,3072]{3,2,1,0:T(8,128)(2,1)S(1)}, u32[]{:S(2)}, u32[]{:S(2)}) collective-permute-start(bf16[1,4,16,3072]{3,2,1,0:T(8,128)(2,1)S(1)} %fusion.38), channel_id=1, source_target_pairs={{0,2},{1,3},{2,0},{3,1},{4,6},{5,7},{6,4},{7,5},{8,10},{9,11},{10,... | collective-permute-start | bytes 1179656 | tf_op jit(solution)/shard_map/ppermute | solution.py:71
  13.8 14.6 %collective-permute-start.2 = (bf16[1,4,16,3072]{3,2,1,0:T(8,128)(2,1)S(1)}, bf16[1,4,16,3072]{3,2,1,0:T(8,128)(2,1)S(1)}, u32[]{:S(2)}, u32[]{:S(2)}) collective-permute-start(bf16[1,4,16,3072]{3,2,1,0:T(8,128)(2,1)S(1)} %fusion.38), channel_id=1, source_target_pairs={{0,1},{1,2},{2,3},{3,0},{4,5},{5,6},{6,7},{7,4},{8,9},{9,10},{10,1... | collective-permute-start | bytes 1179656 | tf_op jit(solution)/shard_map/ppermute | solution.py:71
  45.9 26.9 %all-to-all-start = ((bf16[32,3,4,1024]{3,2,1,0:T(4,128)(2,1)}), bf16[32,3,4,1024]{3,2,1,0:T(4,128)(2,1)S(1)}, u32[]{:S(2)}, u32[]{:S(2)}) async-start(bf16[32,3,4,1024]{3,2,1,0:T(4,128)(2,1)} %copy.36), calls=%async_computation | async-start | bytes 1572864 | tf_op jit(solution)/shard_map/all_to_all | solution.py:205
  91.7 15.8 %all-to-all-start.1 = ((bf16[1,4,32,1024]{3,1,0,2:T(4,128)(2,1)}), bf16[1,4,32,1024]{3,1,0,2:T(4,128)(2,1)S(1)}, u32[]{:S(2)}, u32[]{:S(2)}) async-start(bf16[1,4,32,1024]{3,1,0,2:T(4,128)(2,1)} %copy.40), calls=%async_computation.1 | async-start | bytes 524288 | tf_op jit(solution)/shard_map/all_to_all | solution.py:219
  118.1 2.1 collective-permute-start.3
  118.7 1.4 collective-permute-start.4
  119.4 0.8 collective-permute-start.5
  120.1 29.8 %copy-start.8 = (f32[1,1,3072]{2,0,1:T(1,128)S(1)}, f32[1,1,3072]{2,0,1:T(1,128)}, u32[]{:S(2)}) copy-start(f32[1,1,3072]{2,0,1:T(1,128)} %copy-done.7) | copy-start | bytes 36868
  120.1 29.8 %copy-start.10 = (f32[1,1,3072]{2,0,1:T(1,128)S(1)}, f32[1,1,3072]{2,0,1:T(1,128)}, u32[]{:S(2)}) copy-start(f32[1,1,3072]{2,0,1:T(1,128)} %copy-done.9) | copy-start | bytes 36868
  120.1 29.8 %copy-start.12 = (f32[1,1,3072]{2,0,1:T(1,128)S(1)}, f32[1,1,3072]{2,0,1:T(1,128)}, u32[]{:S(2)}) copy-start(f32[1,1,3072]{2,0,1:T(1,128)} %copy-done.11) | copy-start | bytes 36868
  120.2 29.8 %copy-start.14 = (f32[1,1,3072]{2,0,1:T(1,128)S(1)}, f32[1,1,3072]{2,0,1:T(1,128)}, u32[]{:S(2)}) copy-start(f32[1,1,3072]{2,0,1:T(1,128)} %copy-done.13) | copy-start | bytes 36868
  121.7 27.8 %collective-permute-start.6 = (bf16[1,4,16,3072]{3,2,1,0:T(8,128)(2,1)S(1)}, bf16[1,4,16,3072]{3,2,1,0:T(8,128)(2,1)S(1)}, u32[]{:S(2)}, u32[]{:S(2)}) collective-permute-start(bf16[1,4,16,3072]{3,2,1,0:T(8,128)(2,1)S(1)} %fusion.40), channel_id=1, source_target_pairs={{0,128},{128,0},{1,129},{129,1},{2,130},{130,2},{3,131},{131,3},{4... | collective-permute-start | bytes 1179656 | tf_op jit(solution)/shard_map/ppermute | solution.py:16
  150.2 13.2 %collective-permute-start.7 = (bf16[1,4,16,3072]{3,2,1,0:T(8,128)(2,1)S(1)}, bf16[1,4,16,3072]{3,2,1,0:T(8,128)(2,1)S(1)}, u32[]{:S(2)}, u32[]{:S(2)}) collective-permute-start(bf16[1,4,16,3072]{3,2,1,0:T(8,128)(2,1)S(1)} %fusion.39), channel_id=1, source_target_pairs={{128,131},{129,128},{130,129},{131,130},{132,135},{133,132},{134,1... | collective-permute-start | bytes 1179656 | tf_op jit(solution)/shard_map/ppermute | solution.py:71
  154.5 10.1 %collective-permute-start.8 = (bf16[1,4,16,3072]{3,2,1,0:T(8,128)(2,1)S(1)}, bf16[1,4,16,3072]{3,2,1,0:T(8,128)(2,1)S(1)}, u32[]{:S(2)}, u32[]{:S(2)}) collective-permute-start(bf16[1,4,16,3072]{3,2,1,0:T(8,128)(2,1)S(1)} %fusion.39), channel_id=1, source_target_pairs={{128,130},{129,131},{130,128},{131,129},{132,134},{133,135},{134,1... | collective-permute-start | bytes 1179656 | tf_op jit(solution)/shard_map/ppermute | solution.py:71
  157.5 11.3 %collective-permute-start.9 = (bf16[1,4,16,3072]{3,2,1,0:T(8,128)(2,1)S(1)}, bf16[1,4,16,3072]{3,2,1,0:T(8,128)(2,1)S(1)}, u32[]{:S(2)}, u32[]{:S(2)}) collective-permute-start(bf16[1,4,16,3072]{3,2,1,0:T(8,128)(2,1)S(1)} %fusion.39), channel_id=1, source_target_pairs={{128,129},{129,130},{130,131},{131,128},{132,133},{133,134},{134,1... | collective-permute-start | bytes 1179656 | tf_op jit(solution)/shard_map/ppermute | solution.py:71
  206.9 20.7 %copy-start.21 = (s32[4]{0:T(128)S(1)}, s32[4]{0:T(128)}, u32[]{:S(2)}) copy-start(s32[4]{0:T(128)} %constant.179.clone) | copy-start | bytes 52
  206.9 21.9 %copy-start.20 = (s32[4]{0:T(128)S(1)}, s32[4]{0:T(128)}, u32[]{:S(2)}) copy-start(s32[4]{0:T(128)} %constant.178.clone) | copy-start | bytes 52
  207.0 23.1 %copy-start.17 = (f32[1,3]{1,0:T(1,128)S(1)}, f32[1,3]{1,0:T(1,128)}, u32[]{:S(2)}) copy-start(f32[1,3]{1,0:T(1,128)} %param.24) | copy-start | bytes 40
  223.0 15.1 %all-to-all-start.3 = ((bf16[1,4,32,1024]{3,1,0,2:T(4,128)(2,1)}), bf16[1,4,32,1024]{3,1,0,2:T(4,128)(2,1)S(1)}, u32[]{:S(2)}, u32[]{:S(2)}) async-start(bf16[1,4,32,1024]{3,1,0,2:T(4,128)(2,1)} %copy.52), calls=%async_computation.3 | async-start | bytes 524288 | tf_op jit(solution)/shard_map/all_to_all | solution.py:219
  242.6 14.2 %collective-permute-start.10 = (bf16[1,4,16,3072]{3,2,1,0:T(8,128)(2,1)}, bf16[1,4,16,3072]{3,2,1,0:T(8,128)(2,1)}, u32[]{:S(2)}, u32[]{:S(2)}) collective-permute-start(bf16[1,4,16,3072]{3,2,1,0:T(8,128)(2,1)} %get-tuple-element.11), channel_id=1, source_target_pairs={{128,129},{129,130},{130,131},{131,128},{132,133},{133,134},{134,1... | collective-permute-start | bytes 1179656 | tf_op jit(solution)/shard_map/ppermute | solution.py:71
  244.5 12.3 %collective-permute-start.11 = (bf16[1,4,16,3072]{3,2,1,0:T(8,128)(2,1)}, bf16[1,4,16,3072]{3,2,1,0:T(8,128)(2,1)}, u32[]{:S(2)}, u32[]{:S(2)}) collective-permute-start(bf16[1,4,16,3072]{3,2,1,0:T(8,128)(2,1)} %get-tuple-element.13), channel_id=1, source_target_pairs={{128,130},{129,131},{130,128},{131,129},{132,134},{133,135},{134,1... | collective-permute-start | bytes 1179656 | tf_op jit(solution)/shard_map/ppermute | solution.py:71
  247.8 11.5 %collective-permute-start.12 = (bf16[1,4,16,3072]{3,2,1,0:T(8,128)(2,1)}, bf16[1,4,16,3072]{3,2,1,0:T(8,128)(2,1)}, u32[]{:S(2)}, u32[]{:S(2)}) collective-permute-start(bf16[1,4,16,3072]{3,2,1,0:T(8,128)(2,1)} %get-tuple-element.12), channel_id=1, source_target_pairs={{128,131},{129,128},{130,129},{131,130},{132,135},{133,132},{134,1... | collective-permute-start | bytes 1179656 | tf_op jit(solution)/shard_map/ppermute | solution.py:71
  261.9 7.8 %collective-permute-start.13 = (f32[1,4,16,64]{3,2,1,0:T(8,128)S(1)}, f32[1,4,16,64]{3,2,1,0:T(8,128)S(1)}, u32[]{:S(2)}, u32[]{:S(2)}) collective-permute-start(f32[1,4,16,64]{3,2,1,0:T(8,128)S(1)} %bitcast.212), channel_id=1, source_target_pairs={{128,0},{129,1},{130,131},{131,128},{132,4},{133,5},{134,135},{135... | collective-permute-start | bytes 49160 | tf_op jit(solution)/shard_map/ppermute | solution.py:245
  265.2 6.2 %collective-permute-start.14 = (f32[1,4,16,64]{3,2,1,0:T(8,128)S(1)}, f32[1,4,16,64]{3,2,1,0:T(8,128)S(1)}, u32[]{:S(2)}, u32[]{:S(2)}) collective-permute-start(f32[1,4,16,64]{3,2,1,0:T(8,128)S(1)} %bitcast.213), channel_id=1, source_target_pairs={{128,1},{129,2},{130,128},{131,129},{132,5},{133,6},{134,132},{135... | collective-permute-start | bytes 49160 | tf_op jit(solution)/shard_map/ppermute | solution.py:245
  267.1 4.2 %collective-permute-start.15 = (f32[1,4,16,64]{3,2,1,0:T(8,128)S(1)}, f32[1,4,16,64]{3,2,1,0:T(8,128)S(1)}, u32[]{:S(2)}, u32[]{:S(2)}) collective-permute-start(f32[1,4,16,64]{3,2,1,0:T(8,128)S(1)} %bitcast.214), channel_id=1, source_target_pairs={{128,2},{129,3},{130,129},{131,130},{132,6},{133,7},{134,133},{135... | collective-permute-start | bytes 49160 | tf_op jit(solution)/shard_map/ppermute | solution.py:245
  268.4 3.0 %collective-permute-start.16 = (f32[1,4,16,64]{3,2,1,0:T(8,128)S(1)}, f32[1,4,16,64]{3,2,1,0:T(8,128)S(1)}, u32[]{:S(2)}, u32[]{:S(2)}) collective-permute-start(f32[1,4,16,64]{3,2,1,0:T(8,128)S(1)} %bitcast.215), channel_id=1, source_target_pairs={{128,3},{129,0},{132,7},{133,4},{136,11},{137,8},{140,15},{141,12}... | collective-permute-start | bytes 49160 | tf_op jit(solution)/shard_map/ppermute | solution.py:245
  (11 other events, 135.1 us)
Sparse Core Ops, SparseCore 0:
  14.7 90.9 all-gather.2
where the time goes:
time: 282 us; the launch traced here: 281 us
  starting transfers between devices  76.9 us (27%)
  waiting for transfers between devices  47.4 us (17%)
  local copies, waits for them, and re-layouts  46.8 us (17%)
  matrix products  25.7 us (9%)
  Pallas kernels  24.9 us (9%)
  other arithmetic  24.4 us (9%)
  blocking collectives  18.2 us (6%)
  between operations  16.3 us (6%)
    ppermute x1, starting transfers between devices, from_behind(): return lax.ppermute(value, axis, pairs)  26.5 us
    pallas_call x2, Pallas kernels, attend(): pl.pallas_call(attend_kernel, grid=(2 * patches,), in_specs=[pl.BlockSpec...  24.9 us
    ppermute x12, starting transfers between devices, shift_within(): return lax.ppermute(value, ('section', 'cfg'), pairs)  22.3 us
    dot_general x2, matrix products, run(): jnp.dot(mixed_rows.reshape(-1, width), qkv_full, preferred_element_type=j...  19.5 us
    all_to_all x2, waiting for transfers between devices, run(): lax.all_to_all(attended, 'seq', split_axis=2, concat_axis=0, tiled=True)  18.3 us
    all_to_all x1, blocking collectives, run(): lax.all_to_all(outgoing, 'seq', split_axis=0, concat_axis=3, tiled=True)  18.2 us
    ppermute x12, waiting for transfers between devices, shift_within(): return lax.ppermute(value, ('section', 'cfg'), pairs)  15.6 us
    unnamed x48, local copies, waits for them, and re-layouts  14.5 us
  transfers between devices with their start and end apart: 21, of which 10 were waited for; matrix products, arithmetic and copies ran while one was open for 17% of the time, Pallas kernels for 4%

commit v1 on v0

--- a/solution.py
+++ b/solution.py
@@ -104,7 +104,7 @@
         (((1,), (1,)), ((), ())),
         preferred_element_type=jnp.float32,
     )
-    scores = jnp.where(live_ref[...] > 0, scores, -jnp.inf)
+    scores = scores + live_ref[...]
     row_max = jnp.max(scores, axis=1, keepdims=True)
     weights = jnp.exp(scores - row_max)
     row_sum = jnp.sum(weights, axis=1, keepdims=True)
@@ -171,7 +171,7 @@
     text_limit = lax.dynamic_index_in_dim(text_len, my_sequence, keepdims=False)
     video_limit = lax.dynamic_index_in_dim(video_len, my_sequence // 2, keepdims=False)
     live_keys = jnp.where(row_ids < TEXT, row_ids < text_limit, row_ids - TEXT < video_limit)
-    live_flags = live_keys.astype(jnp.int32)[None, :]
+    live_flags = jnp.where(live_keys, 0.0, -jnp.inf).astype(jnp.float32)[None, :]
     scale_factor = HD ** (-0.5)
 
     row_place = (

time: 282 us -> 282 us (level)
  no operation moved by 1% of the time
where the time goes in v1:
time: 282 us; the launch traced here: 281 us
  starting transfers between devices  76.9 us (27%)
  waiting for transfers between devices  47.4 us (17%)
  local copies, waits for them, and re-layouts  46.8 us (17%)
  matrix products  25.7 us (9%)
  Pallas kernels  24.8 us (9%)
  other arithmetic  24.4 us (9%)
  blocking collectives  18.2 us (6%)
  between operations  16.3 us (6%)
    ppermute x1, starting transfers between devices, from_behind(): return lax.ppermute(value, axis, pairs)  26.5 us
    pallas_call x2, Pallas kernels, attend(): pl.pallas_call(attend_kernel, grid=(2 * patches,), in_specs=[pl.BlockSpec...  24.8 us
    ppermute x12, starting transfers between devices, shift_within(): return lax.ppermute(value, ('section', 'cfg'), pairs)  22.3 us
    dot_general x2, matrix products, run(): jnp.dot(mixed_rows.reshape(-1, width), qkv_full, preferred_element_type=j...  19.5 us
    all_to_all x2, waiting for transfers between devices, run(): lax.all_to_all(attended, 'seq', split_axis=2, concat_axis=0, tiled=True)  18.3 us
    all_to_all x1, blocking collectives, run(): lax.all_to_all(outgoing, 'seq', split_axis=0, concat_axis=3, tiled=True)  18.2 us
    ppermute x12, waiting for transfers between devices, shift_within(): return lax.ppermute(value, ('section', 'cfg'), pairs)  15.6 us
    unnamed x48, local copies, waits for them, and re-layouts  14.5 us
  transfers between devices with their start and end apart: 21, of which 10 were waited for; matrix products, arithmetic and copies ran while one was open for 17% of the time, Pallas kernels for 4%

profile of v1, /device:TPU:1, one launch (start us, length us, event | category | flops | bytes accessed | tf_op | source)
XLA Modules:
  0.0 280.6 jit_solution(3644386847185136882)
XLA Ops:
  15.3 12.7 %copy.31 = bf16[1,3072,3,512]{1,3,2,0:T(8,128)(2,1)} copy(bf16[1,3072,3,512]{3,1,2,0:T(8,128)(2,1)} %param.19) | data formatting | bytes 18874368 | tf_op args[3]
  28.4 9.8 %convolution_bitcast_fusion.3 = f32[4,8,3,4,16,64]{5,4,1,2,3,0:T(8,128)S(1)} fusion(bf16[3,8,64,3072,1,1]{3,2,1,0,5,4:T(8,128)(2,1)} %bitcast.187, s32[]{:T(128)S(6)} %select_n.221, bf16[1,4,16,3072]{3,2,1,0:T(8,128)(2,1)S(1)} %collective-permute-done, bf16[1,4,16,3072]{3,2,1,0:T(8,128)(2,1)S(1)} %collective-permute-done.1, ...), kind=kOutput, calls=%fused_computation.19 | convolution fusion | flops 2428502016 | bytes 12582916 | tf_op jit(solution)/shard_map/dot_general | solution.py:196
  45.9 12.0 %all-to-all-start = ((bf16[32,3,4,1024]{3,2,1,0:T(4,128)(2,1)}), bf16[32,3,4,1024]{3,2,1,0:T(4,128)(2,1)S(1)}, u32[]{:S(2)}, u32[]{:S(2)}) async-start(bf16[32,3,4,1024]{3,2,1,0:T(4,128)(2,1)} %copy.36), calls=%async_computation | async-start | bytes 1572864 | tf_op jit(solution)/shard_map/all_to_all | solution.py:205
  59.2 1.9 select_select_fusion.live_ref
  62.3 10.5 %all-to-all-done = bf16[32,3,4,1024]{3,2,1,0:T(4,128)(2,1)S(1)} async-done(((bf16[32,3,4,1024]{3,2,1,0:T(4,128)(2,1)}), bf16[32,3,4,1024]{3,2,1,0:T(4,128)(2,1)S(1)}, u32[]{:S(2)}, u32[]{:S(2)}) %all-to-all-start) | async-done | bytes 786464 | tf_op jit(solution)/shard_map/all_to_all | solution.py:205
  76.8 12.4 %shard_map.149 = bf16[4,512,64]{2,1,0:T(8,128)(2,1)} custom-call(bf16[4,512,64]{2,1,0:T(8,128)(2,1)} %squeeze.92.query_ref, bf16[2048,64]{1,0:T(8,128)(2,1)} %reshape_squeeze.16.fresh_key_ref, bf16[2048,64]{1,0:T(8,128)(2,1)} %reshape_squeeze.17.fresh_value_ref, bf16[2048,64]{1,0:T(8,128)(2,1)} %get-tuple-element.36.stale_key_ref, ...), custom_call_target="tpu_custom_call" | custom-call | tf_op jit(solution)/shard_map/pallas_call | solution.py:120
  91.6 4.9 %all-to-all-start.1 = ((bf16[1,4,32,1024]{3,1,0,2:T(4,128)(2,1)}), bf16[1,4,32,1024]{3,1,0,2:T(4,128)(2,1)S(1)}, u32[]{:S(2)}, u32[]{:S(2)}) async-start(bf16[1,4,32,1024]{3,1,0,2:T(4,128)(2,1)} %copy.40), calls=%async_computation.1 | async-start | bytes 524288 | tf_op jit(solution)/shard_map/all_to_all | solution.py:219
  96.5 10.9 %all-to-all-done.1 = bf16[1,4,32,1024]{3,1,0,2:T(4,128)(2,1)S(1)} async-done(((bf16[1,4,32,1024]{3,1,0,2:T(4,128)(2,1)}), bf16[1,4,32,1024]{3,1,0,2:T(4,128)(2,1)S(1)}, u32[]{:S(2)}, u32[]{:S(2)}) %all-to-all-start.1) | async-done | bytes 262176 | tf_op jit(solution)/shard_map/all_to_all | solution.py:219
  107.8 4.6 %copy.42 = bf16[1,3072,512]{1,2,0:T(8,128)(2,1)} copy(bf16[1,3072,512]{2,1,0:T(8,128)(2,1)} %all-gather.3.cloned.1.call-done) | data formatting | bytes 6291456 | tf_op jit(solution)/shard_map/all_gather | solution.py:162
  112.5 3.0 %convolution_bitcast_fusion.1 = f32[4,4,16,3072]{3,2,1,0:T(8,128)S(1)} fusion(bf16[4,8,4,16,64]{4,3,2,1,0:T(8,128)(2,1)S(1)} %reshape.441, bf16[3072,8,64,1,1]{0,2,4,1,3:T(8,128)(2,1)} %bitcast.189), kind=kOutput, calls=%fused_computation.1 | convolution fusion | flops 805306368 | bytes 6553600 | tf_op jit(solution)/shard_map/sgpqe,dge->spqd/dot_general | solution.py:222
  115.4 1.6 copy-done.4
  121.6 26.5 %collective-permute-start.6 = (bf16[1,4,16,3072]{3,2,1,0:T(8,128)(2,1)S(1)}, bf16[1,4,16,3072]{3,2,1,0:T(8,128)(2,1)S(1)}, u32[]{:S(2)}, u32[]{:S(2)}) collective-permute-start(bf16[1,4,16,3072]{3,2,1,0:T(8,128)(2,1)S(1)} %fusion.40), channel_id=1, source_target_pairs={{0,128},{128,0},{1,129},{129,1},{2,130},{130,2},{3,131},{131,3},{4... | collective-permute-start | bytes 1179656 | tf_op jit(solution)/shard_map/ppermute | solution.py:16
  150.2 4.3 %collective-permute-start.7 = (bf16[1,4,16,3072]{3,2,1,0:T(8,128)(2,1)S(1)}, bf16[1,4,16,3072]{3,2,1,0:T(8,128)(2,1)S(1)}, u32[]{:S(2)}, u32[]{:S(2)}) collective-permute-start(bf16[1,4,16,3072]{3,2,1,0:T(8,128)(2,1)S(1)} %fusion.39), channel_id=1, source_target_pairs={{128,131},{129,128},{130,129},{131,130},{132,135},{133,132},{134,1... | collective-permute-start | bytes 1179656 | tf_op jit(solution)/shard_map/ppermute | solution.py:71
  154.5 2.9 %collective-permute-start.8 = (bf16[1,4,16,3072]{3,2,1,0:T(8,128)(2,1)S(1)}, bf16[1,4,16,3072]{3,2,1,0:T(8,128)(2,1)S(1)}, u32[]{:S(2)}, u32[]{:S(2)}) collective-permute-start(bf16[1,4,16,3072]{3,2,1,0:T(8,128)(2,1)S(1)} %fusion.39), channel_id=1, source_target_pairs={{128,130},{129,131},{130,128},{131,129},{132,134},{133,135},{134,1... | collective-permute-start | bytes 1179656 | tf_op jit(solution)/shard_map/ppermute | solution.py:71
  157.4 2.1 collective-permute-start.9
  159.6 3.8 %collective-permute-done.7 = bf16[1,4,16,3072]{3,2,1,0:T(8,128)(2,1)S(1)} collective-permute-done((bf16[1,4,16,3072]{3,2,1,0:T(8,128)(2,1)S(1)}, bf16[1,4,16,3072]{3,2,1,0:T(8,128)(2,1)S(1)}, u32[]{:S(2)}, u32[]{:S(2)}) %collective-permute-start.7) | collective-permute-done | bytes 393248 | tf_op jit(solution)/shard_map/ppermute | solution.py:71
  164.6 4.1 %collective-permute-done.9 = bf16[1,4,16,3072]{3,2,1,0:T(8,128)(2,1)S(1)} collective-permute-done((bf16[1,4,16,3072]{3,2,1,0:T(8,128)(2,1)S(1)}, bf16[1,4,16,3072]{3,2,1,0:T(8,128)(2,1)S(1)}, u32[]{:S(2)}, u32[]{:S(2)}) %collective-permute-start.9) | collective-permute-done | bytes 393248 | tf_op jit(solution)/shard_map/ppermute | solution.py:71
  168.7 9.7 %convolution_bitcast_fusion.2 = f32[4,8,3,4,16,64]{5,4,1,3,0,2:T(8,128)S(1)} fusion(bf16[3,8,64,3072,1,1]{3,2,1,5,4,0:T(8,128)(2,1)} %bitcast.188, s32[]{:T(128)S(6)} %select_n.221, bf16[1,4,16,3072]{3,2,1,0:T(8,128)(2,1)S(1)} %collective-permute-done.7, bf16[1,4,16,3072]{3,2,1,0:T(8,128)(2,1)S(1)} %collective-permute-done.8, ...), kind=kOutput, calls=%fused_computation.18 | convolution fusion | flops 2428502016 | bytes 12582916 | tf_op jit(solution)/shard_map/dot_general | solution.py:196
  185.8 18.2 %all_to_all.60 = bf16[32,3,4,1024]{3,2,1,0:T(4,128)(2,1)S(1)} all-to-all(bf16[32,3,4,1024]{3,2,1,0:T(4,128)(2,1)S(1)} %copy.48), channel_id=1, replica_groups=mesh['section'=2,'seq'=32,'cfg'=4] {'seq'}, dimensions={0} | all-to-all | bytes 1572864 | tf_op jit(solution)/shard_map/all_to_all | solution.py:205
  208.1 12.4 %shard_map.150 = bf16[4,512,64]{2,1,0:T(8,128)(2,1)} custom-call(bf16[4,512,64]{2,1,0:T(8,128)(2,1)} %squeeze.99.query_ref, bf16[2048,64]{1,0:T(8,128)(2,1)} %reshape_squeeze.18.fresh_key_ref, bf16[2048,64]{1,0:T(8,128)(2,1)} %reshape_squeeze.19.fresh_value_ref, bf16[2048,64]{1,0:T(8,128)(2,1)} %get-tuple-element.36.stale_key_ref, ...), custom_call_target="tpu_custom_call" | custom-call | tf_op jit(solution)/shard_map/pallas_call | solution.py:120
  222.8 4.7 %all-to-all-start.3 = ((bf16[1,4,32,1024]{3,1,0,2:T(4,128)(2,1)}), bf16[1,4,32,1024]{3,1,0,2:T(4,128)(2,1)S(1)}, u32[]{:S(2)}, u32[]{:S(2)}) async-start(bf16[1,4,32,1024]{3,1,0,2:T(4,128)(2,1)} %copy.52), calls=%async_computation.3 | async-start | bytes 524288 | tf_op jit(solution)/shard_map/all_to_all | solution.py:219
  230.6 7.3 %all-to-all-done.3 = bf16[1,4,32,1024]{3,1,0,2:T(4,128)(2,1)S(1)} async-done(((bf16[1,4,32,1024]{3,1,0,2:T(4,128)(2,1)}), bf16[1,4,32,1024]{3,1,0,2:T(4,128)(2,1)S(1)}, u32[]{:S(2)}, u32[]{:S(2)}) %all-to-all-start.3) | async-done | bytes 262176 | tf_op jit(solution)/shard_map/all_to_all | solution.py:219
  238.3 2.9 %convolution_bitcast_fusion = f32[4,4,16,3072]{3,2,1,0:T(8,128)S(1)} fusion(bf16[4,8,4,16,64]{4,3,2,1,0:T(8,128)(2,1)S(1)} %reshape.442, bf16[3072,8,64,1,1]{0,2,4,1,3:T(8,128)(2,1)} %bitcast.190), kind=kOutput, calls=%fused_computation | convolution fusion | flops 805306368 | bytes 6553600 | tf_op jit(solution)/shard_map/sgpqe,dge->spqd/dot_general | solution.py:222
  242.4 1.9 collective-permute-start.10
  244.3 3.4 %collective-permute-start.11 = (bf16[1,4,16,3072]{3,2,1,0:T(8,128)(2,1)}, bf16[1,4,16,3072]{3,2,1,0:T(8,128)(2,1)}, u32[]{:S(2)}, u32[]{:S(2)}) collective-permute-start(bf16[1,4,16,3072]{3,2,1,0:T(8,128)(2,1)} %get-tuple-element.13), channel_id=1, source_target_pairs={{128,130},{129,131},{130,128},{131,129},{132,134},{133,135},{134,1... | collective-permute-start | bytes 1179656 | tf_op jit(solution)/shard_map/ppermute | solution.py:71
  247.7 3.5 %collective-permute-start.12 = (bf16[1,4,16,3072]{3,2,1,0:T(8,128)(2,1)}, bf16[1,4,16,3072]{3,2,1,0:T(8,128)(2,1)}, u32[]{:S(2)}, u32[]{:S(2)}) collective-permute-start(bf16[1,4,16,3072]{3,2,1,0:T(8,128)(2,1)} %get-tuple-element.12), channel_id=1, source_target_pairs={{128,131},{129,128},{130,129},{131,130},{132,135},{133,132},{134,1... | collective-permute-start | bytes 1179656 | tf_op jit(solution)/shard_map/ppermute | solution.py:71
  252.7 3.9 %collective-permute-done.10 = bf16[1,4,16,3072]{3,2,1,0:T(8,128)(2,1)} collective-permute-done((bf16[1,4,16,3072]{3,2,1,0:T(8,128)(2,1)}, bf16[1,4,16,3072]{3,2,1,0:T(8,128)(2,1)}, u32[]{:S(2)}, u32[]{:S(2)}) %collective-permute-start.10) | collective-permute-done | bytes 393248 | tf_op jit(solution)/shard_map/ppermute | solution.py:71
  256.7 2.5 collective-permute-done.12
  259.2 1.9 convert_reduce_fusion.2
  261.7 1.9 collective-permute-start.13
  265.0 1.9 collective-permute-start.14
  271.2 2.5 fusion.57
  (169 shorter events, 57.3 us)
Async XLA Ops:
  7.2 254.2 %copy-start = (bf16[3072,64]{0,1:T(8,128)(2,1)S(1)}, bf16[3072,64]{0,1:T(8,128)(2,1)}, u32[]{:S(2)}) copy-start(bf16[3072,64]{0,1:T(8,128)(2,1)} %param.23) | copy-start | bytes 1179652
  7.2 100.6 %all-gather.3.cloned.1.call-start = ((), (), s32[]{:S(2)}) async-start(), calls=%async_computation.4 | async-start | bytes 3244032 | tf_op jit(solution)/shard_map/all_gather | solution.py:162
  8.7 19.3 %copy-start.9 = (f32[1,1,3072]{2,0,1:T(1,128)}, f32[1,1,3072]{2,0,1:T(1,128)S(1)}, u32[]{:S(2)}) copy-start(f32[1,1,3072]{2,0,1:T(1,128)S(1)} %get-tuple-element.43) | copy-start | bytes 36868
  8.7 19.3 %copy-start.11 = (f32[1,1,3072]{2,0,1:T(1,128)}, f32[1,1,3072]{2,0,1:T(1,128)S(1)}, u32[]{:S(2)}) copy-start(f32[1,1,3072]{2,0,1:T(1,128)S(1)} %get-tuple-element.45) | copy-start | bytes 36868
  8.7 19.3 %copy-start.13 = (f32[1,1,3072]{2,0,1:T(1,128)}, f32[1,1,3072]{2,0,1:T(1,128)S(1)}, u32[]{:S(2)}) copy-start(f32[1,1,3072]{2,0,1:T(1,128)S(1)} %get-tuple-element.46) | copy-start | bytes 36868
  12.4 16.0 %collective-permute-start = (bf16[1,4,16,3072]{3,2,1,0:T(8,128)(2,1)S(1)}, bf16[1,4,16,3072]{3,2,1,0:T(8,128)(2,1)S(1)}, u32[]{:S(2)}, u32[]{:S(2)}) collective-permute-start(bf16[1,4,16,3072]{3,2,1,0:T(8,128)(2,1)S(1)} %fusion.38), channel_id=1, source_target_pairs={{0,3},{1,0},{2,1},{3,2},{4,7},{5,4},{6,5},{7,6},{8,11},{9,8},{10,9... | collective-permute-start | bytes 1179656 | tf_op jit(solution)/shard_map/ppermute | solution.py:71
  13.1 15.3 %collective-permute-start.1 = (bf16[1,4,16,3072]{3,2,1,0:T(8,128)(2,1)S(1)}, bf16[1,4,16,3072]{3,2,1,0:T(8,128)(2,1)S(1)}, u32[]{:S(2)}, u32[]{:S(2)}) collective-permute-start(bf16[1,4,16,3072]{3,2,1,0:T(8,128)(2,1)S(1)} %fusion.38), channel_id=1, source_target_pairs={{0,2},{1,3},{2,0},{3,1},{4,6},{5,7},{6,4},{7,5},{8,10},{9,11},{10,... | collective-permute-start | bytes 1179656 | tf_op jit(solution)/shard_map/ppermute | solution.py:71
  13.8 14.6 %collective-permute-start.2 = (bf16[1,4,16,3072]{3,2,1,0:T(8,128)(2,1)S(1)}, bf16[1,4,16,3072]{3,2,1,0:T(8,128)(2,1)S(1)}, u32[]{:S(2)}, u32[]{:S(2)}) collective-permute-start(bf16[1,4,16,3072]{3,2,1,0:T(8,128)(2,1)S(1)} %fusion.38), channel_id=1, source_target_pairs={{0,1},{1,2},{2,3},{3,0},{4,5},{5,6},{6,7},{7,4},{8,9},{9,10},{10,1... | collective-permute-start | bytes 1179656 | tf_op jit(solution)/shard_map/ppermute | solution.py:71
  45.9 26.9 %all-to-all-start = ((bf16[32,3,4,1024]{3,2,1,0:T(4,128)(2,1)}), bf16[32,3,4,1024]{3,2,1,0:T(4,128)(2,1)S(1)}, u32[]{:S(2)}, u32[]{:S(2)}) async-start(bf16[32,3,4,1024]{3,2,1,0:T(4,128)(2,1)} %copy.36), calls=%async_computation | async-start | bytes 1572864 | tf_op jit(solution)/shard_map/all_to_all | solution.py:205
  91.6 15.9 %all-to-all-start.1 = ((bf16[1,4,32,1024]{3,1,0,2:T(4,128)(2,1)}), bf16[1,4,32,1024]{3,1,0,2:T(4,128)(2,1)S(1)}, u32[]{:S(2)}, u32[]{:S(2)}) async-start(bf16[1,4,32,1024]{3,1,0,2:T(4,128)(2,1)} %copy.40), calls=%async_computation.1 | async-start | bytes 524288 | tf_op jit(solution)/shard_map/all_to_all | solution.py:219
  118.0 2.1 collective-permute-start.3
  118.7 1.4 collective-permute-start.4
  119.4 0.8 collective-permute-start.5
  120.1 29.8 %copy-start.8 = (f32[1,1,3072]{2,0,1:T(1,128)S(1)}, f32[1,1,3072]{2,0,1:T(1,128)}, u32[]{:S(2)}) copy-start(f32[1,1,3072]{2,0,1:T(1,128)} %copy-done.7) | copy-start | bytes 36868
  120.1 29.8 %copy-start.10 = (f32[1,1,3072]{2,0,1:T(1,128)S(1)}, f32[1,1,3072]{2,0,1:T(1,128)}, u32[]{:S(2)}) copy-start(f32[1,1,3072]{2,0,1:T(1,128)} %copy-done.9) | copy-start | bytes 36868
  120.1 29.8 %copy-start.12 = (f32[1,1,3072]{2,0,1:T(1,128)S(1)}, f32[1,1,3072]{2,0,1:T(1,128)}, u32[]{:S(2)}) copy-start(f32[1,1,3072]{2,0,1:T(1,128)} %copy-done.11) | copy-start | bytes 36868
  120.1 29.8 %copy-start.14 = (f32[1,1,3072]{2,0,1:T(1,128)S(1)}, f32[1,1,3072]{2,0,1:T(1,128)}, u32[]{:S(2)}) copy-start(f32[1,1,3072]{2,0,1:T(1,128)} %copy-done.13) | copy-start | bytes 36868
  121.6 27.8 %collective-permute-start.6 = (bf16[1,4,16,3072]{3,2,1,0:T(8,128)(2,1)S(1)}, bf16[1,4,16,3072]{3,2,1,0:T(8,128)(2,1)S(1)}, u32[]{:S(2)}, u32[]{:S(2)}) collective-permute-start(bf16[1,4,16,3072]{3,2,1,0:T(8,128)(2,1)S(1)} %fusion.40), channel_id=1, source_target_pairs={{0,128},{128,0},{1,129},{129,1},{2,130},{130,2},{3,131},{131,3},{4... | collective-permute-start | bytes 1179656 | tf_op jit(solution)/shard_map/ppermute | solution.py:16
  150.2 13.2 %collective-permute-start.7 = (bf16[1,4,16,3072]{3,2,1,0:T(8,128)(2,1)S(1)}, bf16[1,4,16,3072]{3,2,1,0:T(8,128)(2,1)S(1)}, u32[]{:S(2)}, u32[]{:S(2)}) collective-permute-start(bf16[1,4,16,3072]{3,2,1,0:T(8,128)(2,1)S(1)} %fusion.39), channel_id=1, source_target_pairs={{128,131},{129,128},{130,129},{131,130},{132,135},{133,132},{134,1... | collective-permute-start | bytes 1179656 | tf_op jit(solution)/shard_map/ppermute | solution.py:71
  154.5 10.1 %collective-permute-start.8 = (bf16[1,4,16,3072]{3,2,1,0:T(8,128)(2,1)S(1)}, bf16[1,4,16,3072]{3,2,1,0:T(8,128)(2,1)S(1)}, u32[]{:S(2)}, u32[]{:S(2)}) collective-permute-start(bf16[1,4,16,3072]{3,2,1,0:T(8,128)(2,1)S(1)} %fusion.39), channel_id=1, source_target_pairs={{128,130},{129,131},{130,128},{131,129},{132,134},{133,135},{134,1... | collective-permute-start | bytes 1179656 | tf_op jit(solution)/shard_map/ppermute | solution.py:71
  157.4 11.3 %collective-permute-start.9 = (bf16[1,4,16,3072]{3,2,1,0:T(8,128)(2,1)S(1)}, bf16[1,4,16,3072]{3,2,1,0:T(8,128)(2,1)S(1)}, u32[]{:S(2)}, u32[]{:S(2)}) collective-permute-start(bf16[1,4,16,3072]{3,2,1,0:T(8,128)(2,1)S(1)} %fusion.39), channel_id=1, source_target_pairs={{128,129},{129,130},{130,131},{131,128},{132,133},{133,134},{134,1... | collective-permute-start | bytes 1179656 | tf_op jit(solution)/shard_map/ppermute | solution.py:71
  206.9 20.7 %copy-start.21 = (s32[4]{0:T(128)S(1)}, s32[4]{0:T(128)}, u32[]{:S(2)}) copy-start(s32[4]{0:T(128)} %constant.181.clone) | copy-start | bytes 52
  206.9 21.8 %copy-start.20 = (s32[4]{0:T(128)S(1)}, s32[4]{0:T(128)}, u32[]{:S(2)}) copy-start(s32[4]{0:T(128)} %constant.180.clone) | copy-start | bytes 52
  206.9 23.0 %copy-start.17 = (f32[1,3]{1,0:T(1,128)S(1)}, f32[1,3]{1,0:T(1,128)}, u32[]{:S(2)}) copy-start(f32[1,3]{1,0:T(1,128)} %param.24) | copy-start | bytes 40
  222.8 15.1 %all-to-all-start.3 = ((bf16[1,4,32,1024]{3,1,0,2:T(4,128)(2,1)}), bf16[1,4,32,1024]{3,1,0,2:T(4,128)(2,1)S(1)}, u32[]{:S(2)}, u32[]{:S(2)}) async-start(bf16[1,4,32,1024]{3,1,0,2:T(4,128)(2,1)} %copy.52), calls=%async_computation.3 | async-start | bytes 524288 | tf_op jit(solution)/shard_map/all_to_all | solution.py:219
  242.4 14.2 %collective-permute-start.10 = (bf16[1,4,16,3072]{3,2,1,0:T(8,128)(2,1)}, bf16[1,4,16,3072]{3,2,1,0:T(8,128)(2,1)}, u32[]{:S(2)}, u32[]{:S(2)}) collective-permute-start(bf16[1,4,16,3072]{3,2,1,0:T(8,128)(2,1)} %get-tuple-element.11), channel_id=1, source_target_pairs={{128,129},{129,130},{130,131},{131,128},{132,133},{133,134},{134,1... | collective-permute-start | bytes 1179656 | tf_op jit(solution)/shard_map/ppermute | solution.py:71
  244.3 12.3 %collective-permute-start.11 = (bf16[1,4,16,3072]{3,2,1,0:T(8,128)(2,1)}, bf16[1,4,16,3072]{3,2,1,0:T(8,128)(2,1)}, u32[]{:S(2)}, u32[]{:S(2)}) collective-permute-start(bf16[1,4,16,3072]{3,2,1,0:T(8,128)(2,1)} %get-tuple-element.13), channel_id=1, source_target_pairs={{128,130},{129,131},{130,128},{131,129},{132,134},{133,135},{134,1... | collective-permute-start | bytes 1179656 | tf_op jit(solution)/shard_map/ppermute | solution.py:71
  247.7 11.5 %collective-permute-start.12 = (bf16[1,4,16,3072]{3,2,1,0:T(8,128)(2,1)}, bf16[1,4,16,3072]{3,2,1,0:T(8,128)(2,1)}, u32[]{:S(2)}, u32[]{:S(2)}) collective-permute-start(bf16[1,4,16,3072]{3,2,1,0:T(8,128)(2,1)} %get-tuple-element.12), channel_id=1, source_target_pairs={{128,131},{129,128},{130,129},{131,130},{132,135},{133,132},{134,1... | collective-permute-start | bytes 1179656 | tf_op jit(solution)/shard_map/ppermute | solution.py:71
  261.7 7.8 %collective-permute-start.13 = (f32[1,4,16,64]{3,2,1,0:T(8,128)S(1)}, f32[1,4,16,64]{3,2,1,0:T(8,128)S(1)}, u32[]{:S(2)}, u32[]{:S(2)}) collective-permute-start(f32[1,4,16,64]{3,2,1,0:T(8,128)S(1)} %bitcast.212), channel_id=1, source_target_pairs={{128,0},{129,1},{130,131},{131,128},{132,4},{133,5},{134,135},{135... | collective-permute-start | bytes 49160 | tf_op jit(solution)/shard_map/ppermute | solution.py:245
  265.0 6.2 %collective-permute-start.14 = (f32[1,4,16,64]{3,2,1,0:T(8,128)S(1)}, f32[1,4,16,64]{3,2,1,0:T(8,128)S(1)}, u32[]{:S(2)}, u32[]{:S(2)}) collective-permute-start(f32[1,4,16,64]{3,2,1,0:T(8,128)S(1)} %bitcast.213), channel_id=1, source_target_pairs={{128,1},{129,2},{130,128},{131,129},{132,5},{133,6},{134,132},{135... | collective-permute-start | bytes 49160 | tf_op jit(solution)/shard_map/ppermute | solution.py:245
  266.9 4.2 %collective-permute-start.15 = (f32[1,4,16,64]{3,2,1,0:T(8,128)S(1)}, f32[1,4,16,64]{3,2,1,0:T(8,128)S(1)}, u32[]{:S(2)}, u32[]{:S(2)}) collective-permute-start(f32[1,4,16,64]{3,2,1,0:T(8,128)S(1)} %bitcast.214), channel_id=1, source_target_pairs={{128,2},{129,3},{130,129},{131,130},{132,6},{133,7},{134,133},{135... | collective-permute-start | bytes 49160 | tf_op jit(solution)/shard_map/ppermute | solution.py:245
  268.2 3.0 %collective-permute-start.16 = (f32[1,4,16,64]{3,2,1,0:T(8,128)S(1)}, f32[1,4,16,64]{3,2,1,0:T(8,128)S(1)}, u32[]{:S(2)}, u32[]{:S(2)}) collective-permute-start(f32[1,4,16,64]{3,2,1,0:T(8,128)S(1)} %bitcast.215), channel_id=1, source_target_pairs={{128,3},{129,0},{132,7},{133,4},{136,11},{137,8},{140,15},{141,12}... | collective-permute-start | bytes 49160 | tf_op jit(solution)/shard_map/ppermute | solution.py:245
  (11 other events, 135.1 us)
Sparse Core Ops, SparseCore 0:
  14.7 90.8 all-gather.2
